TPU v7x, 256 devices: a whole 4x4x8 slice. The times are simulated.
256 devices in a mesh: section: 16 (over x, z_lo), expert: 16 (over y, z_hi, core).
Axes of the slice: x: 4, y: 4, z: 8 (z_hi: 2, z_lo: 4; z = z_hi * 4 + z_lo), core: 2. Of those that a mesh axis runs over, the one named last changes fastest.
Arguments:
- stream: bfloat16 [16, 256, 4096], P('section', 'expert'), may hold values from -6 to 6
- queries: bfloat16 [16, 256, 4096], P('section', None, 'expert'), may hold values from -6 to 6
- keyvals: bfloat16 [16, 4096, 512], P('section', 'expert'), may hold values from -6 to 6
- w_out: bfloat16 [16, 4096, 4096], P('section', 'expert'), may hold values from -0.5 to 0.5
- norm_gain: float32 [16, 4096], P('section'), may hold values from 0.5 to 1.5
- w_gate: bfloat16 [16, 4096, 6144], P('section', None, 'expert'), may hold values from -0.09375 to 0.09375
- w_up: bfloat16 [16, 4096, 6144], P('section', None, 'expert'), may hold values from -0.09375 to 0.09375
- w_down: bfloat16 [16, 6144, 4096], P('section', 'expert'), may hold values from -0.3125 to 0.3125
- routes: int32 [16, 256, 2], P('section'), may hold values from 0 to 3, all different within a row; in each aligned block of 16 rows (0 to 15, 16 to 31, ..., all dimensions but the last counted through in order) at most 12 rows name the same one
- gate_scores: float32 [16, 256, 2], P('section'), may hold values from 0.05 to 20
Outputs:
- passed: bfloat16 [16, 256, 4096], P('section', 'expert')
Inputs may be any that keep to these rules, and one draw needn't show every extreme that they name: `routes`: each row names 2 different experts. In each aligned block of 16 rows (the tokens of one device) no expert is named by more than 12 rows.
All inputs are finite; a program needn't handle non-finite values.
Results may differ from a plain program's by a relative error of at most 0.02.
Values may be sent and summed in bfloat16 or wider, within the bound.
No kernel may reach another device: no remote copies, remote signals or barrier semaphores. Data moves between devices by JAX's collectives and lax.ppermute only.
A program may use at most 64 MiB of HBM per device.

v0:
```python
import math
import jax
import jax.numpy as jnp
from jax import lax
from jax.sharding import PartitionSpec as P

HD = 128
FF = 1536
QHEADS = 32
KVHEADS = 2
CTX = 4096
MB = 256


def shifted(block, axis, distance):
    devices = range(lax.axis_size(axis))
    route = [((i - distance) % len(devices), i) for i in devices]
    return lax.ppermute(block, axis, route)


def body(stream, queries, keyvals, w_out, norm_gain, w_gate, w_up, w_down, routes, gate_scores):
    my_index = lax.axis_index("expert")
    devices = lax.axis_size("expert")
    tok_rows = stream.shape[1]
    residual = stream[0]
    query_all = queries[0]
    proj_out = w_out[0]
    gain = norm_gain[0]
    gate_w = w_gate[0]
    up_w = w_up[0]
    down_w = w_down[0]
    heads_here = query_all.shape[1] // HD
    group = QHEADS // KVHEADS
    scale = 1.0 / math.sqrt(HD)
    query_pos = CTX - MB + jnp.arange(MB, dtype=jnp.int32)
    piece = lax.all_gather(keyvals[0], "expert", axis=0, tiled=True)
    tops = jnp.full((heads_here, MB), -1e30, jnp.float32)
    totals = jnp.zeros((heads_here, MB), jnp.float32)
    sums = jnp.zeros((heads_here, MB, HD), jnp.float32)
    key_pos = jnp.arange(piece.shape[0], dtype=jnp.int32)
    visible = key_pos[None, :] <= query_pos[:, None]
    new_tops = []
    new_totals = []
    new_sums = []
    for head in range(heads_here):
        column = (my_index * heads_here + head) // group * (2 * HD)
        keys = lax.dynamic_slice_in_dim(piece, column, HD, 1)
        values = lax.dynamic_slice_in_dim(piece, column + HD, HD, 1)
        query = query_all[:, head * HD : (head + 1) * HD]
        score = (
            lax.dot_general(
                query, keys, (((1,), (1,)), ((), ())), preferred_element_type=jnp.float32
            )
            * scale
        )
        top_new = jnp.maximum(tops[head], jnp.max(jnp.where(visible, score, -1e30), axis=1))
        weight = jnp.where(visible, jnp.exp(score - top_new[:, None]), 0.0)
        factor = jnp.exp(tops[head] - top_new)
        new_tops.append(top_new)
        new_totals.append(totals[head] * factor + jnp.sum(weight, axis=1))
        new_sums.append(
            sums[head] * factor[:, None]
            + jnp.dot(weight.astype(jnp.bfloat16), values, preferred_element_type=jnp.float32)
        )
    totals = jnp.stack(new_totals)
    sums = jnp.stack(new_sums)
    heads = (sums / totals[:, :, None]).astype(jnp.bfloat16)
    heads = jnp.transpose(heads, (1, 0, 2)).reshape(MB, heads_here * HD)
    attended = lax.psum_scatter(
        jnp.dot(heads, proj_out, preferred_element_type=jnp.float32).astype(jnp.bfloat16),
        "expert",
        scatter_dimension=0,
        tiled=True,
    ).astype(jnp.float32)
    middle = residual.astype(jnp.float32) + attended
    normed = (
        middle * lax.rsqrt(jnp.mean(middle * middle, axis=1, keepdims=True) + 1e-06) * gain
    ).astype(jnp.bfloat16)
    split = FF // gate_w.shape[1]
    experts_count = devices // split
    chosen = lax.dynamic_slice_in_dim(routes[0], my_index * tok_rows, tok_rows, 0)
    scores_in = lax.dynamic_slice_in_dim(gate_scores[0], my_index * tok_rows, tok_rows, 0)
    onehot = chosen[:, :, None] == jnp.arange(experts_count, dtype=jnp.int32)[None, None, :]
    share = jnp.sum(jnp.where(onehot, scores_in[:, :, None], 0.0), axis=1) / jnp.sum(
        scores_in, axis=1, keepdims=True
    )
    share_dev = jnp.repeat(share, split, axis=1)
    outgoing_rows = jnp.broadcast_to(normed[None], (devices, tok_rows, normed.shape[1]))
    rows = lax.all_to_all(outgoing_rows, "expert", split_axis=0, concat_axis=0, tiled=True)
    flat = rows.reshape(-1, rows.shape[-1])
    gate = jnp.dot(flat, gate_w, preferred_element_type=jnp.float32)
    upper = jnp.dot(flat, up_w, preferred_element_type=jnp.float32)
    activated = (jax.nn.silu(gate) * upper).astype(jnp.bfloat16)
    computed = (
        jnp.dot(activated, down_w, preferred_element_type=jnp.float32)
        .astype(jnp.bfloat16)
        .reshape(rows.shape)
    )
    picked = lax.all_to_all(computed, "expert", split_axis=0, concat_axis=0, tiled=True)
    mixed = jnp.einsum(
        "td,dtk->tk", share_dev, picked.astype(jnp.float32), precision=lax.Precision.HIGHEST
    )
    layer_out = (middle + mixed).astype(jnp.bfloat16)
    return shifted(layer_out[None], "section", 1)


def solution(mesh):
    return jax.shard_map(
        body,
        mesh=mesh,
        in_specs=(
            P("section", "expert", None),
            P("section", None, "expert"),
            P("section", "expert", None),
            P("section", "expert", None),
            P("section", None),
            P("section", None, "expert"),
            P("section", None, "expert"),
            P("section", "expert", None),
            P("section", None, None),
            P("section", None, None),
        ),
        out_specs=P("section", "expert", None),
        check_vma=False,
    )
```

profile of v0, /device:TPU:8, one launch (start us, length us, event | category | flops | bytes accessed | tf_op | source)
XLA Modules:
  0.0 325.5 jit_solution(16367630738279816033)
XLA Ops:
  6.5 0.7 all-gather.3.cloned.1.call-update
  7.4 82.3 %all-gather.3.cloned.1.call-done = bf16[1,4096,512]{2,1,0:T(8,128)(2,1)} async-done(((bf16[1,256,512]{2,1,0:T(8,128)(2,1)}), bf16[1,4096,512]{2,1,0:T(8,128)(2,1)}) %all-gather.3.cloned.1.call-update) | async-done | bytes 4194320 | tf_op jit(solution)/shard_map/all_gather | solution.py:36
  89.7 2.3 select_reduce_fusion.1
  92.0 0.2 copy-done.8
  92.2 1.7 fusion.2
  93.9 1.1 fusion.4
  95.0 1.0 fusion.27
  96.1 1.0 fusion.33
  97.1 0.5 copy-done.1
  97.6 2.1 convolution_convert_fusion.1
  99.7 83.5 %reduce-scatter.2.cloned.1.call-done = bf16[16,4096]{1,0:T(8,128)(2,1)} async-done(((bf16[256,4096]{1,0:T(8,128)(2,1)}), bf16[16,4096]{1,0:T(8,128)(2,1)}) %reduce-scatter.2.cloned.1.call-update) | async-done | bytes 131088 | tf_op jit(solution)/shard_map/reduce_scatter | solution.py:69
  183.3 1.2 multiply_reduce_fusion
  184.5 1.0 multiply_convert_fusion
  185.5 0.2 broadcast_in_dim.53
  185.8 34.0 %all_to_all.10 = bf16[16,16,4096]{2,1,0:T(8,128)(2,1)S(1)} all-to-all(bf16[16,16,4096]{2,1,0:T(8,128)(2,1)S(1)} %broadcast_in_dim.53), channel_id=1, replica_groups=mesh['section'=16,'expert'=16] {'expert'}, dimensions={0} | all-to-all | bytes 4194304 | tf_op jit(solution)/shard_map/all_to_all | solution.py:89
  219.8 1.3 copy-done.2
  221.1 2.0 fusion.9
  223.1 6.4 %convolution_convert_fusion = bf16[256,4096]{1,0:T(8,128)(2,1)} fusion(bf16[1,384,4096]{2,1,0:T(8,128)(2,1)S(1)} %copy-done, bf16[256,4096]{1,0:T(8,128)(2,1)} %bitcast.77, bf16[1,4096,384]{2,1,0:T(8,128)(2,1)} %param.16, f32[256,384]{1,0:T(8,128)} %fusion.9), kind=kOutput, calls=%fused_computation.4 | convolution fusion | flops 1612251136 | bytes 10878976 | tf_op jit(solution)/shard_map/dot_general | solution.py:95
  229.5 7.2 %all-to-all-start.1 = ((bf16[16,16,4096]{2,1,0:T(8,128)(2,1)}), bf16[16,16,4096]{2,1,0:T(8,128)(2,1)}, u32[]{:S(2)}, u32[]{:S(2)}) async-start(bf16[16,16,4096]{2,1,0:T(8,128)(2,1)} %bitcast.75), calls=%async_computation.2 | async-start | bytes 4194304 | tf_op jit(solution)/shard_map/all_to_all | solution.py:99
  236.9 29.0 %all-to-all-done.1 = bf16[16,16,4096]{2,1,0:T(8,128)(2,1)} async-done(((bf16[16,16,4096]{2,1,0:T(8,128)(2,1)}), bf16[16,16,4096]{2,1,0:T(8,128)(2,1)}, u32[]{:S(2)}, u32[]{:S(2)}) %all-to-all-start.1) | async-done | bytes 2097184 | tf_op jit(solution)/shard_map/all_to_all | solution.py:99
  266.0 4.6 %fusion.12 = f32[16,1,4096]{2,1,0:T(1,128)S(1)} fusion(f32[16,16,1]{1,2,0:T(1,128)S(1)} %copy.15, bf16[16,16,4096]{2,1,0:T(8,128)(2,1)} %all-to-all-done.1), kind=kOutput, calls=%fused_computation.21 | convolution fusion | flops 12582912 | bytes 2360320 | tf_op jit(solution)/shard_map/td,dtk->tk/dot_general | solution.py:100
  270.7 42.1 %collective-permute-start = (bf16[1,16,4096]{2,1,0:T(8,128)(2,1)S(1)}, bf16[1,16,4096]{2,1,0:T(8,128)(2,1)S(1)}, u32[]{:S(2)}, u32[]{:S(2)}) collective-permute-start(bf16[1,16,4096]{2,1,0:T(8,128)(2,1)S(1)} %fusion.54), channel_id=1, source_target_pairs={{240,0},{0,16},{16,32},{32,48},{48,64},{64,80},{80,96},{96,112},{1... | collective-permute-start | bytes 393224 | tf_op jit(solution)/shard_map/ppermute | solution.py:18
  312.8 5.1 %collective-permute-done = bf16[1,16,4096]{2,1,0:T(8,128)(2,1)S(1)} collective-permute-done((bf16[1,16,4096]{2,1,0:T(8,128)(2,1)S(1)}, bf16[1,16,4096]{2,1,0:T(8,128)(2,1)S(1)}, u32[]{:S(2)}, u32[]{:S(2)}) %collective-permute-start) | collective-permute-done | bytes 131104 | tf_op jit(solution)/shard_map/ppermute | solution.py:18
  318.0 0.7 copy.24
  (36 shorter events, 0.6 us)
Async XLA Ops:
  6.5 216.6 %copy-start = (bf16[1,384,4096]{2,1,0:T(8,128)(2,1)S(1)}, bf16[1,384,4096]{2,1,0:T(8,128)(2,1)}, u32[]{:S(2)}) copy-start(bf16[1,384,4096]{2,1,0:T(8,128)(2,1)} %param.17) | copy-start | bytes 9437188
  6.5 85.5 %copy-start.10 = (bf16[1,256,256]{2,1,0:T(8,128)(2,1)S(1)}, bf16[1,256,256]{2,1,0:T(8,128)(2,1)}, u32[]{:S(2)}) copy-start(bf16[1,256,256]{2,1,0:T(8,128)(2,1)} %param.11) | copy-start | bytes 393220
  6.5 83.1 %all-gather.3.cloned.1.call-start = ((), (), s32[]{:S(2)}) async-start(), calls=%async_computation.4 | async-start | bytes 4456448 | tf_op jit(solution)/shard_map/all_gather | solution.py:36
  7.3 176.0 %reduce-scatter.2.cloned.1.call-start = ((), (), s32[]{:S(2)}) async-start(), calls=%async_computation.3 | async-start | bytes 2228224 | tf_op jit(solution)/shard_map/reduce_scatter | solution.py:69
  89.7 2.5 copy-start.8
  96.1 1.6 copy-start.1
  97.1 86.2 %copy-start.3 = (bf16[1,16,4096]{2,1,0:T(8,128)(2,1)S(1)}, bf16[1,16,4096]{2,1,0:T(8,128)(2,1)}, u32[]{:S(2)}) copy-start(bf16[1,16,4096]{2,1,0:T(8,128)(2,1)} %param.10) | copy-start | bytes 393220
  97.1 87.4 %copy-start.5 = (f32[1,4096]{1,0:T(1,128)S(1)}, f32[1,4096]{1,0:T(1,128)}, u32[]{:S(2)}) copy-start(f32[1,4096]{1,0:T(1,128)} %param.14) | copy-start | bytes 49156
  183.3 37.8 %copy-start.9 = (bf16[1,4096,384]{2,1,0:T(8,128)(2,1)S(1)}, bf16[1,4096,384]{2,1,0:T(8,128)(2,1)}, u32[]{:S(2)}) copy-start(bf16[1,4096,384]{2,1,0:T(8,128)(2,1)} %param.15) | copy-start | bytes 9437188
  219.8 1.3 copy-start.2
  229.5 7.2 %copy-start.6 = (f32[1,256,2]{1,2,0:T(2,128)S(1)}, f32[1,256,2]{1,2,0:T(2,128)}, u32[]{:S(2)}) copy-start(f32[1,256,2]{1,2,0:T(2,128)} %param.19) | copy-start | bytes 6148
  229.5 7.3 %copy-start.7 = (s32[1,256,2]{1,2,0:T(2,128)S(1)}, s32[1,256,2]{1,2,0:T(2,128)}, u32[]{:S(2)}) copy-start(s32[1,256,2]{1,2,0:T(2,128)} %param.18) | copy-start | bytes 6148
  229.5 41.0 %copy-start.4 = (bf16[16,4096]{1,0:T(8,128)(2,1)S(1)}, bf16[16,4096]{1,0:T(8,128)(2,1)}, u32[]{:S(2)}) copy-start(bf16[16,4096]{1,0:T(8,128)(2,1)} %reduce-scatter.2.cloned.1.call-done) | copy-start | bytes 393220
  229.5 36.5 %all-to-all-start.1 = ((bf16[16,16,4096]{2,1,0:T(8,128)(2,1)}), bf16[16,16,4096]{2,1,0:T(8,128)(2,1)}, u32[]{:S(2)}, u32[]{:S(2)}) async-start(bf16[16,16,4096]{2,1,0:T(8,128)(2,1)} %bitcast.75), calls=%async_computation.2 | async-start | bytes 4194304 | tf_op jit(solution)/shard_map/all_to_all | solution.py:99
  270.7 47.2 %collective-permute-start = (bf16[1,16,4096]{2,1,0:T(8,128)(2,1)S(1)}, bf16[1,16,4096]{2,1,0:T(8,128)(2,1)S(1)}, u32[]{:S(2)}, u32[]{:S(2)}) collective-permute-start(bf16[1,16,4096]{2,1,0:T(8,128)(2,1)S(1)} %fusion.54), channel_id=1, source_target_pairs={{240,0},{0,16},{16,32},{32,48},{48,64},{64,80},{80,96},{96,112},{1... | collective-permute-start | bytes 393224 | tf_op jit(solution)/shard_map/ppermute | solution.py:18
Sparse Core Ops, SparseCore 0:
  10.0 79.6 all-gather.2
  99.9 83.3 reduce-scatter.1
where the time goes:
time: 326 us; the launch traced here: 325 us
  waiting for transfers between devices  201 us (62%)
  starting transfers between devices  49.3 us (15%)
  blocking collectives  34 us (10%)
  matrix products  21.1 us (6%)
  between operations  13.6 us (4%)
  other arithmetic  3.66 us (1%)
    reduce_scatter x1, waiting for transfers between devices, body(): lax.psum_scatter(jnp.dot(heads, proj_out, preferred_element_type=jnp.floa...  83.5 us
    all_gather x1, waiting for transfers between devices, body(): piece = lax.all_gather(keyvals[0], 'expert', axis=0, tiled=True)  82.3 us
    ppermute x1, starting transfers between devices, shifted(): return lax.ppermute(block, axis, route)  42.1 us
    all_to_all x1, blocking collectives, body(): lax.all_to_all(outgoing_rows, 'expert', split_axis=0, concat_axis=0, tile...  34 us
    all_to_all x1, waiting for transfers between devices, body(): lax.all_to_all(computed, 'expert', split_axis=0, concat_axis=0, tiled=True)  29 us
    all_to_all x1, starting transfers between devices, body(): lax.all_to_all(computed, 'expert', split_axis=0, concat_axis=0, tiled=True)  7.17 us
  transfers between devices with their start and end apart: 4, of which 4 were waited for; matrix products, arithmetic and copies ran while one was open for 0% of the time, Pallas kernels for 0%

commit v1 on v0

--- a/solution.py
+++ b/solution.py
@@ -1,8 +1,10 @@
+import functools
 import math
 import jax
 import jax.numpy as jnp
 from jax import lax
 from jax.sharding import PartitionSpec as P
+from jax.lax import all_to_all, axis_size
 
 HD = 128
 FF = 1536
@@ -10,6 +12,17 @@
 KVHEADS = 2
 CTX = 4096
 MB = 256
+
+
+def numbers_reach(page, axis_tag):
+    heard = jnp.stack(tuple((page for _ in range(axis_size(axis_tag)))), axis=0)
+    e_next = jnp.concatenate(
+        all_to_all(heard, concat_axis=0, axis_name=axis_tag, split_axis=0), axis=0
+    )
+    return e_next
+
+
+lay_tracks = functools.partial(numbers_reach, axis_tag="expert")
 
 
 def shifted(block, axis, distance):
@@ -33,7 +46,7 @@
     group = QHEADS // KVHEADS
     scale = 1.0 / math.sqrt(HD)
     query_pos = CTX - MB + jnp.arange(MB, dtype=jnp.int32)
-    piece = lax.all_gather(keyvals[0], "expert", axis=0, tiled=True)
+    piece = lay_tracks(keyvals[0])
     tops = jnp.full((heads_here, MB), -1e30, jnp.float32)
     totals = jnp.zeros((heads_here, MB), jnp.float32)
     sums = jnp.zeros((heads_here, MB, HD), jnp.float32)

time: 326 us -> 362 us (1.11)
  starting transfers between devices: 49.3 us -> 65.2 us
  waiting for transfers between devices: 201 us -> 213 us
  matrix products: 21.1 us -> 24.8 us
    all_gather x1 -> x0, waiting for transfers between devices: 82.3 us -> none  [body(): piece = lax.all_gather(keyvals[0], 'expert', axis=0, tiled=True)]
    all_to_all x0 -> x1, waiting for transfers between devices: none -> 61.5 us  [numbers_reach(): all_to_all(heard, concat_axis=0, axis_name=axis_tag, split_axis=0)]
    reduce_scatter x1, waiting for transfers between devices: 83.5 us -> 120 us  [body(): lax.psum_scatter(jnp.dot(heads, proj_out, preferred_element_type=jnp.floa...]
    all_to_all x0 -> x1, starting transfers between devices: none -> 11.7 us  [numbers_reach(): all_to_all(heard, concat_axis=0, axis_name=axis_tag, split_axis=0)]
    ppermute x1, starting transfers between devices: 42.1 us -> 46.3 us  [shifted(): return lax.ppermute(block, axis, route)]
where the time goes in v1:
time: 362 us; the launch traced here: 360 us
  waiting for transfers between devices  213 us (59%)
  starting transfers between devices  65.2 us (18%)
  blocking collectives  33.9 us (9%)
  matrix products  24.8 us (7%)
  between operations  13.6 us (4%)
  local copies, waits for them, and re-layouts  5.84 us (2%)
  other arithmetic  3.65 us (1%)
    reduce_scatter x1, waiting for transfers between devices, body(): lax.psum_scatter(jnp.dot(heads, proj_out, preferred_element_type=jnp.floa...  120 us
    all_to_all x1, waiting for transfers between devices, numbers_reach(): all_to_all(heard, concat_axis=0, axis_name=axis_tag, split_axis=0)  61.5 us
    ppermute x1, starting transfers between devices, shifted(): return lax.ppermute(block, axis, route)  46.3 us
    all_to_all x1, blocking collectives, body(): lax.all_to_all(outgoing_rows, 'expert', split_axis=0, concat_axis=0, tile...  33.9 us
    all_to_all x1, waiting for transfers between devices, body(): lax.all_to_all(computed, 'expert', split_axis=0, concat_axis=0, tiled=True)  29 us
    all_to_all x1, starting transfers between devices, numbers_reach(): all_to_all(heard, concat_axis=0, axis_name=axis_tag, split_axis=0)  11.7 us
  transfers between devices with their start and end apart: 4, of which 4 were waited for; matrix products, arithmetic and copies ran while one was open for 0% of the time, Pallas kernels for 0%

profile of v1, /device:TPU:8, one launch (start us, length us, event | category | flops | bytes accessed | tf_op | source)
XLA Modules:
  0.0 360.5 jit_solution(6107939913456682592)
XLA Ops:
  6.5 3.5 stack.17
  10.0 11.7 %all-to-all-start = ((bf16[16,256,512]{2,1,0:T(8,128)(2,1)}), bf16[16,256,512]{2,1,0:T(8,128)(2,1)}, u32[]{:S(2)}, u32[]{:S(2)}) async-start(bf16[16,256,512]{2,1,0:T(8,128)(2,1)} %stack.17), calls=%async_computation | async-start | bytes 8388608 | tf_op jit(solution)/shard_map/all_to_all | solution.py:20
  21.8 61.5 %all-to-all-done = bf16[16,256,512]{2,1,0:T(8,128)(2,1)} async-done(((bf16[16,256,512]{2,1,0:T(8,128)(2,1)}), bf16[16,256,512]{2,1,0:T(8,128)(2,1)}, u32[]{:S(2)}, u32[]{:S(2)}) %all-to-all-start) | async-done | bytes 4194336 | tf_op jit(solution)/shard_map/all_to_all | solution.py:20
  83.3 2.1 select_reduce_fusion.1
  85.4 3.0 fusion.2
  88.4 1.1 fusion.4
  89.5 2.2 fusion.27
  91.8 2.4 fusion.33
  94.2 2.1 convolution_convert_fusion.1
  96.4 120.4 %reduce-scatter.2.cloned.1.call-done = bf16[16,4096]{1,0:T(8,128)(2,1)} async-done(((bf16[256,4096]{1,0:T(8,128)(2,1)}), bf16[16,4096]{1,0:T(8,128)(2,1)}) %reduce-scatter.2.cloned.1.call-update) | async-done | bytes 131088 | tf_op jit(solution)/shard_map/reduce_scatter | solution.py:82
  216.8 1.2 multiply_reduce_fusion
  218.0 1.0 multiply_convert_fusion
  219.0 0.2 broadcast_in_dim.53
  219.2 33.9 %all_to_all.15 = bf16[16,16,4096]{2,1,0:T(8,128)(2,1)S(1)} all-to-all(bf16[16,16,4096]{2,1,0:T(8,128)(2,1)S(1)} %broadcast_in_dim.53), channel_id=1, replica_groups=mesh['section'=16,'expert'=16] {'expert'}, dimensions={0} | all-to-all | bytes 4194304 | tf_op jit(solution)/shard_map/all_to_all | solution.py:102
  253.2 1.3 copy-done.2
  254.5 2.1 fusion.9
  256.5 6.4 %convolution_convert_fusion = bf16[256,4096]{1,0:T(8,128)(2,1)} fusion(bf16[1,384,4096]{2,1,0:T(8,128)(2,1)S(1)} %copy-done, bf16[256,4096]{1,0:T(8,128)(2,1)} %bitcast.63, bf16[1,4096,384]{2,1,0:T(8,128)(2,1)} %param.16, f32[256,384]{1,0:T(8,128)} %fusion.9), kind=kOutput, calls=%fused_computation.4 | convolution fusion | flops 1612251136 | bytes 10878976 | tf_op jit(solution)/shard_map/dot_general | solution.py:108
  262.9 7.2 %all-to-all-start.2 = ((bf16[16,16,4096]{2,1,0:T(8,128)(2,1)}), bf16[16,16,4096]{2,1,0:T(8,128)(2,1)}, u32[]{:S(2)}, u32[]{:S(2)}) async-start(bf16[16,16,4096]{2,1,0:T(8,128)(2,1)} %bitcast.61), calls=%async_computation.3 | async-start | bytes 4194304 | tf_op jit(solution)/shard_map/all_to_all | solution.py:112
  270.4 29.0 %all-to-all-done.2 = bf16[16,16,4096]{2,1,0:T(8,128)(2,1)} async-done(((bf16[16,16,4096]{2,1,0:T(8,128)(2,1)}), bf16[16,16,4096]{2,1,0:T(8,128)(2,1)}, u32[]{:S(2)}, u32[]{:S(2)}) %all-to-all-start.2) | async-done | bytes 2097184 | tf_op jit(solution)/shard_map/all_to_all | solution.py:112
  299.4 4.6 %fusion.12 = f32[16,1,4096]{2,1,0:T(1,128)S(1)} fusion(f32[16,16,1]{1,2,0:T(1,128)S(1)} %copy.15, bf16[16,16,4096]{2,1,0:T(8,128)(2,1)} %all-to-all-done.2), kind=kOutput, calls=%fused_computation.21 | convolution fusion | flops 12582912 | bytes 2360320 | tf_op jit(solution)/shard_map/td,dtk->tk/dot_general | solution.py:113
  304.0 0.2 fusion.50
  304.1 46.3 %collective-permute-start = (bf16[1,16,4096]{2,1,0:T(8,128)(2,1)S(1)}, bf16[1,16,4096]{2,1,0:T(8,128)(2,1)S(1)}, u32[]{:S(2)}, u32[]{:S(2)}) collective-permute-start(bf16[1,16,4096]{2,1,0:T(8,128)(2,1)S(1)} %fusion.50), channel_id=1, source_target_pairs={{240,0},{0,16},{16,32},{32,48},{48,64},{64,80},{80,96},{96,112},{1... | collective-permute-start | bytes 393224 | tf_op jit(solution)/shard_map/ppermute | solution.py:31
  350.4 2.5 collective-permute-done
  353.0 0.7 copy.24
  (34 shorter events, 0.4 us)
Async XLA Ops:
  6.5 250.0 %copy-start = (bf16[1,384,4096]{2,1,0:T(8,128)(2,1)S(1)}, bf16[1,384,4096]{2,1,0:T(8,128)(2,1)}, u32[]{:S(2)}) copy-start(bf16[1,384,4096]{2,1,0:T(8,128)(2,1)} %param.17) | copy-start | bytes 9437188
  10.0 73.2 %copy-start.9 = (bf16[1,256,256]{2,1,0:T(8,128)(2,1)S(1)}, bf16[1,256,256]{2,1,0:T(8,128)(2,1)}, u32[]{:S(2)}) copy-start(bf16[1,256,256]{2,1,0:T(8,128)(2,1)} %param.11) | copy-start | bytes 393220
  10.0 73.2 %all-to-all-start = ((bf16[16,256,512]{2,1,0:T(8,128)(2,1)}), bf16[16,256,512]{2,1,0:T(8,128)(2,1)}, u32[]{:S(2)}, u32[]{:S(2)}) async-start(bf16[16,256,512]{2,1,0:T(8,128)(2,1)} %stack.17), calls=%async_computation | async-start | bytes 8388608 | tf_op jit(solution)/shard_map/all_to_all | solution.py:20
  21.7 195.1 %reduce-scatter.2.cloned.1.call-start = ((), (), s32[]{:S(2)}) async-start(), calls=%async_computation.4 | async-start | bytes 2228224 | tf_op jit(solution)/shard_map/reduce_scatter | solution.py:82
  91.8 2.5 copy-start.1
  94.2 122.6 %copy-start.3 = (bf16[1,16,4096]{2,1,0:T(8,128)(2,1)S(1)}, bf16[1,16,4096]{2,1,0:T(8,128)(2,1)}, u32[]{:S(2)}) copy-start(bf16[1,16,4096]{2,1,0:T(8,128)(2,1)} %param.10) | copy-start | bytes 393220
  94.2 123.8 %copy-start.5 = (f32[1,4096]{1,0:T(1,128)S(1)}, f32[1,4096]{1,0:T(1,128)}, u32[]{:S(2)}) copy-start(f32[1,4096]{1,0:T(1,128)} %param.14) | copy-start | bytes 49156
  216.8 37.7 %copy-start.8 = (bf16[1,4096,384]{2,1,0:T(8,128)(2,1)S(1)}, bf16[1,4096,384]{2,1,0:T(8,128)(2,1)}, u32[]{:S(2)}) copy-start(bf16[1,4096,384]{2,1,0:T(8,128)(2,1)} %param.15) | copy-start | bytes 9437188
  253.2 1.3 copy-start.2
  262.9 7.2 %copy-start.6 = (f32[1,256,2]{1,2,0:T(2,128)S(1)}, f32[1,256,2]{1,2,0:T(2,128)}, u32[]{:S(2)}) copy-start(f32[1,256,2]{1,2,0:T(2,128)} %param.19) | copy-start | bytes 6148
  262.9 7.3 %copy-start.7 = (s32[1,256,2]{1,2,0:T(2,128)S(1)}, s32[1,256,2]{1,2,0:T(2,128)}, u32[]{:S(2)}) copy-start(s32[1,256,2]{1,2,0:T(2,128)} %param.18) | copy-start | bytes 6148
  262.9 41.1 %copy-start.4 = (bf16[16,4096]{1,0:T(8,128)(2,1)S(1)}, bf16[16,4096]{1,0:T(8,128)(2,1)}, u32[]{:S(2)}) copy-start(bf16[16,4096]{1,0:T(8,128)(2,1)} %reduce-scatter.2.cloned.1.call-done) | copy-start | bytes 393220
  262.9 36.5 %all-to-all-start.2 = ((bf16[16,16,4096]{2,1,0:T(8,128)(2,1)}), bf16[16,16,4096]{2,1,0:T(8,128)(2,1)}, u32[]{:S(2)}, u32[]{:S(2)}) async-start(bf16[16,16,4096]{2,1,0:T(8,128)(2,1)} %bitcast.61), calls=%async_computation.3 | async-start | bytes 4194304 | tf_op jit(solution)/shard_map/all_to_all | solution.py:112
  304.1 48.8 %collective-permute-start = (bf16[1,16,4096]{2,1,0:T(8,128)(2,1)S(1)}, bf16[1,16,4096]{2,1,0:T(8,128)(2,1)S(1)}, u32[]{:S(2)}, u32[]{:S(2)}) collective-permute-start(bf16[1,16,4096]{2,1,0:T(8,128)(2,1)S(1)} %fusion.50), channel_id=1, source_target_pairs={{240,0},{0,16},{16,32},{32,48},{48,64},{64,80},{80,96},{96,112},{1... | collective-permute-start | bytes 393224 | tf_op jit(solution)/shard_map/ppermute | solution.py:31
Sparse Core Ops, SparseCore 0:
  96.5 120.2 reduce-scatter.1
